TPU v7x, 32 devices: a whole 2x2x4 slice. The times are simulated.
32 devices in a mesh: col: 8 (over y, x, core), row: 4 (over z).
Axes of the slice: x: 2, y: 2, z: 4, core: 2. Of those that a mesh axis runs over, the one named last changes fastest.
Arguments:
- p_blocks: bfloat16 [4, 72, 4096], P('row', 'col'), may hold values from -0.5390625 to 0.5390625
- p_slots: int32 [4, 72], P('row', 'col'), may hold values from 0 to 18, as said below
- out_slots: int32 [4, 104], P('row', 'col'), may hold values from 0 to 18, as said below
Outputs:
- purified: float32 [4, 104, 4096], P('row', 'col')
Inputs may be any that keep to these rules, and one draw needn't show every extreme that they name: `p_slots`: on each device the used slots (entries below 18) come first and name distinct positions; the remaining slots hold 18. Each device uses between half of its 9 slots (rounded up) and all of them, and some device uses all. `out_slots`: on each device the used slots (entries below 18) come first and name distinct positions; the remaining slots hold 18. Each device uses between half of its 13 slots (rounded up) and all of them, and some device uses all.
All inputs are finite; a program needn't handle non-finite values.
Results may differ from a plain program's by a relative error of at most 0.0003.
Values may be sent and summed in bfloat16 or wider, within the bound.
No kernel may reach another device: no remote copies, remote signals or barrier semaphores. Data moves between devices by JAX's collectives and lax.ppermute only.
A program may use at most 192 MiB of HBM per device.

v0:
```python
import jax
import jax.numpy as jnp
from jax import lax
from jax.sharding import PartitionSpec as P

BLK = 64
COLS_DEV = 3


def on_device(p_blocks, p_slots, out_slots):
    n_row = lax.axis_size("row")
    n_col = lax.axis_size("col")
    capacity = p_slots.shape[1]
    block_edge = BLK
    area = block_edge * block_edge
    rows_dev = COLS_DEV * n_col // n_row
    cells = rows_dev * COLS_DEV
    blocks_total = rows_dev * n_row
    width = COLS_DEV * block_edge
    height = rows_dev * block_edge
    own_ids = p_slots[0]
    id_row = jnp.zeros((1, area), jnp.bfloat16)
    id_row = id_row.at[0, :capacity].set(own_ids.astype(jnp.bfloat16))
    payload = jnp.concatenate([p_blocks[0], id_row], axis=0)
    down = lax.all_gather(payload, "row", axis=0, tiled=False)
    down_ids = down[:, capacity, :capacity].astype(jnp.int32)
    down_row = jnp.arange(n_row, dtype=jnp.int32)[:, None] * rows_dev + down_ids // COLS_DEV
    down_index = jnp.where(
        down_ids < cells, down_row * COLS_DEV + down_ids % COLS_DEV, blocks_total * COLS_DEV
    )
    column_grid = jnp.zeros((blocks_total * COLS_DEV, area), jnp.bfloat16)
    column_grid = column_grid.at[down_index.reshape(-1)].set(
        down[:, :capacity].reshape(n_row * capacity, area), mode="drop"
    )
    column_panel = (
        column_grid.reshape(blocks_total, COLS_DEV, block_edge, block_edge)
        .transpose(0, 2, 1, 3)
        .reshape(blocks_total * block_edge, width)
    )
    across = lax.all_gather(payload, "col", axis=0, tiled=False)
    across_ids = across[:, capacity, :capacity].astype(jnp.int32)
    across_col = jnp.arange(n_col, dtype=jnp.int32)[:, None] * COLS_DEV + across_ids % COLS_DEV
    across_index = jnp.where(
        across_ids < cells,
        across_ids // COLS_DEV * blocks_total + across_col,
        rows_dev * blocks_total,
    )
    row_grid = jnp.zeros((rows_dev * blocks_total, area), jnp.bfloat16)
    row_grid = row_grid.at[across_index.reshape(-1)].set(
        across[:, :capacity].reshape(n_col * capacity, area), mode="drop"
    )
    row_panel = (
        row_grid.reshape(rows_dev, blocks_total, block_edge, block_edge)
        .transpose(0, 2, 1, 3)
        .reshape(height, blocks_total * block_edge)
    )
    square = jnp.dot(row_panel, column_panel, preferred_element_type=jnp.float32)
    square_panel = lax.all_gather(square, "row", axis=0, tiled=True)
    cube = jnp.dot(
        row_panel.astype(jnp.float32),
        square_panel,
        precision=lax.Precision.HIGHEST,
        preferred_element_type=jnp.float32,
    )
    combined = 3.0 * square - 2.0 * cube
    new_grid = combined.reshape(rows_dev, block_edge, COLS_DEV, block_edge).transpose(0, 2, 1, 3)
    new_grid = new_grid.reshape(cells, area)
    out_ids = out_slots[0]
    picked = new_grid[jnp.minimum(out_ids, cells - 1)]
    picked = jnp.where((out_ids < cells)[:, None], picked, jnp.zeros_like(picked))
    return picked[None]


def solution(mesh):
    in_specs = (P("row", "col", None), P("row", "col"), P("row", "col"))
    out_specs = P("row", "col", None)
    return jax.shard_map(
        on_device, mesh=mesh, in_specs=in_specs, out_specs=out_specs, check_vma=False
    )
```

profile of v0, /device:TPU:0, one launch (start us, length us, event | category | flops | bytes accessed | tf_op | source)
XLA Modules:
  0.0 100.4 jit_solution(6214441134641464494)
XLA Ops:
  6.5 0.0 all-gather.6.cloned.1.call-start
  6.5 0.6 compare_reduce_fusion.4
  7.2 1.3 %broadcast_select_fusion = bf16[1,9]{1,0:T(2,128)(2,1)S(1)} fusion(pred[]{:T(512)} %compare_reduce_fusion.4, s32[1,9]{1,0:T(1,128)} %param.6), kind=kLoop, calls=%fused_computation.34 | loop fusion | flops 18 | bytes 55 | tf_op jit(solution)/shard_map/select.3
  8.5 0.9 fusion.7
  9.4 12.4 %all-gather.2 = bf16[8,10,4096]{2,1,0:T(8,128)(2,1)S(1)} all-gather(bf16[1,10,4096]{2,1,0:T(8,128)(2,1)S(1)} %fusion.7), channel_id=2, replica_groups=mesh['col'=8,'row'=4] {'col'}, dimensions={0}, use_global_device_ids=true | all-gather | bytes 737280 | tf_op jit(solution)/shard_map/all_gather | solution.py:40
  21.9 16.3 %all-gather.3 = bf16[4,10,4096]{2,1,0:T(8,128)(2,1)S(1)} all-gather(bf16[1,10,4096]{2,1,0:T(8,128)(2,1)S(1)} %fusion.7), channel_id=3, replica_groups=mesh['col'=8,'row'=4] {'row'}, dimensions={0}, use_global_device_ids=true | all-gather | bytes 409600 | tf_op jit(solution)/shard_map/all_gather | solution.py:25
  38.3 0.0 copy-start
  38.3 0.8 copy-done
  39.1 0.5 compare_reduce_fusion.2
  39.6 0.1 div.35
  39.7 0.1 rem.56
  39.8 0.1 lt.92
  39.9 0.1 ne.104
  40.0 0.1 add.140
  40.0 0.1 add.141
  40.1 0.3 reshape.316
  40.4 1.8 %scatter_custom_fusion = bf16[144,4096]{1,0:T(8,128)(2,1)S(1)} fusion(s32[72]{0:T(128)S(1)} %fusion.12, bf16[72,4096]{1,0:T(8,128)(2,1)S(1)} %reshape.316, bf16[]{:T(256)} %constant.75.clone.1), kind=kCustom, calls=%fused_computation.5 | custom fusion | bytes 1179650 | tf_op jit(solution)/shard_map/scatter | solution.py:49
  42.2 2.6 %reshape.297 = bf16[6,24,64,64]{3,2,1,0:T(8,128)(2,1)S(1)} reshape(bf16[144,4096]{1,0:T(8,128)(2,1)S(1)} %scatter_custom_fusion) | data formatting | bytes 2359296 | tf_op jit(solution)/shard_map/reshape | solution.py:53
  44.8 2.9 %copy.12 = bf16[6,64,24,64]{3,2,1,0:T(8,128)(2,1)} copy(bf16[6,64,24,64]{3,1,2,0:T(8,128)(2,1)S(1)} %bitcast.34) | data formatting | bytes 2359296 | tf_op jit(solution)/shard_map/transpose | solution.py:54
  47.7 0.0 copy-start.2
  47.7 0.0 copy-start.1
  47.7 3.5 %reshape.298 = bf16[384,1536]{1,0:T(8,128)(2,1)S(1)} reshape(bf16[6,64,24,64]{3,2,1,0:T(8,128)(2,1)} %copy.12) | data formatting | bytes 2359296 | tf_op jit(solution)/shard_map/reshape | solution.py:55
  51.3 0.1 div.37
  51.3 0.1 rem.60
  51.4 0.0 copy-done.2
  51.4 0.1 lt.97
  51.5 0.1 ne.109
  51.6 0.1 add.146
  51.7 0.1 add.147
  51.8 0.0 copy-done.1
  51.8 0.1 reshape.324
  51.9 1.2 %scatter_custom_fusion.1 = bf16[72,4096]{1,0:T(8,128)(2,1)S(1)} fusion(s32[36]{0:T(128)S(1)} %fusion.13, bf16[36,4096]{1,0:T(8,128)(2,1)S(1)} %reshape.324, bf16[]{:T(256)} %constant.75.clone.1), kind=kCustom, calls=%fused_computation.7 | custom fusion | bytes 589826 | tf_op jit(solution)/shard_map/scatter | solution.py:32
  53.1 1.3 %reshape.300 = bf16[24,3,64,64]{3,2,1,0:T(8,128)(2,1)S(1)} reshape(bf16[72,4096]{1,0:T(8,128)(2,1)S(1)} %scatter_custom_fusion.1) | data formatting | bytes 1179648 | tf_op jit(solution)/shard_map/reshape | solution.py:36
  54.4 1.3 %copy.13 = bf16[24,64,3,64]{1,0,3,2:T(8,128)(2,1)S(1)} copy(bf16[24,64,3,64]{3,1,2,0:T(8,128)(2,1)S(1)} %bitcast.35) | data formatting | bytes 1179648 | tf_op jit(solution)/shard_map/transpose | solution.py:37
  55.7 0.7 reshape.301
  56.4 0.0 copy-start.3
  56.4 1.3 %fusion.15 = f32[384,192]{0,1:T(8,128)} fusion(bf16[384,1536]{1,0:T(8,128)(2,1)S(1)} %reshape.298, bf16[1536,192]{0,1:T(8,128)(2,1)S(1)} %reshape.301), kind=kOutput, calls=%fused_computation.44 | convolution fusion | flops 226492416 | bytes 2064384 | tf_op jit(solution)/shard_map/dot_general | solution.py:57
  57.7 0.0 all-gather.6.cloned.1.call-update
  57.7 0.0 copy-done.3
  57.8 30.9 %all-gather.6.cloned.1.call-done = f32[1536,192]{0,1:T(8,128)} async-done(((f32[384,192]{0,1:T(8,128)}), f32[1536,192]{0,1:T(8,128)}) %all-gather.6.cloned.1.call-update) | async-done | bytes 1179664 | tf_op jit(solution)/shard_map/all_gather | solution.py:58
  88.7 2.6 %fusion = f32[384,192]{0,1:T(8,128)S(1)} fusion(bf16[384,1536]{1,0:T(8,128)(2,1)S(1)} %reshape.298, f32[1536,192]{0,1:T(8,128)} %all-gather.6.cloned.1.call-done, f32[384,192]{0,1:T(8,128)} %fusion.15), kind=kOutput, calls=%fused_computation.4 | convolution fusion | flops 1359175680 | bytes 2949120 | tf_op jit(solution)/shard_map/dot_general | solution.py:59
  91.3 0.2 reshape.302
  91.4 0.3 copy.14
  91.7 0.2 reshape.303
  91.9 0.6 gather_fusion
  92.5 0.1 bitcast_select_fusion
  92.6 0.9 copy.15
  (10 shorter events, 0.2 us)
Async XLA Ops:
  6.5 82.2 %all-gather.6.cloned.1.call-start = ((), (), s32[]{:S(2)}) async-start(), calls=%async_computation | async-start | bytes 1474560 | tf_op jit(solution)/shard_map/all_gather | solution.py:58
  38.3 0.8 copy-start
  47.7 3.7 %copy-start.2 = (pred[4,9]{1,0:T(4,128)(4,1)S(1)}, pred[4,9]{1,0:T(4,128)(4,1)}, u32[]{:S(2)}) copy-start(pred[4,9]{1,0:T(4,128)(4,1)} %get-tuple-element.22) | copy-start | bytes 112
  47.7 4.0 %copy-start.1 = (bf16[4,10,4096]{2,1,0:T(8,128)(2,1)S(1)}, bf16[4,10,4096]{2,1,0:T(8,128)(2,1)}, u32[]{:S(2)}) copy-start(bf16[4,10,4096]{2,1,0:T(8,128)(2,1)} %copy-done) | copy-start | bytes 983044
  56.4 1.3 %copy-start.3 = (s32[1,13]{1,0:T(1,128)S(1)}, s32[1,13]{1,0:T(1,128)}, u32[]{:S(2)}) copy-start(s32[1,13]{1,0:T(1,128)} %param.7) | copy-start | bytes 160
Sparse Core Ops, SparseCore 0:
  57.9 30.7 all-gather.5
where the time goes:
time: 101 us; the launch traced here: 100 us
  waiting for transfers between devices  30.9 us (31%)
  blocking collectives  28.8 us (29%)
  local copies, waits for them, and re-layouts  19.6 us (19%)
  between operations  13.6 us (13%)
  matrix products  3.83 us (4%)
  other arithmetic  3.67 us (4%)
    all_gather x1, waiting for transfers between devices, on_device(): square_panel = lax.all_gather(square, 'row', axis=0, tiled=True)  30.9 us
    all_gather x1, blocking collectives, on_device(): down = lax.all_gather(payload, 'row', axis=0, tiled=False)  16.3 us
    all_gather x1, blocking collectives, on_device(): across = lax.all_gather(payload, 'col', axis=0, tiled=False)  12.4 us
    reshape x1, local copies, waits for them, and re-layouts, on_device(): row_panel = row_grid.reshape(rows_dev, blocks_total, block_edge, block_ed...  3.5 us
    transpose x1, local copies, waits for them, and re-layouts, on_device(): row_panel = row_grid.reshape(rows_dev, blocks_total, block_edge, block_ed...  2.94 us
    reshape x1, local copies, waits for them, and re-layouts, on_device(): row_grid.reshape(rows_dev, blocks_total, block_edge, block_edge)  2.57 us
    dot_general x1, matrix products, on_device(): jnp.dot(row_panel.astype(jnp.float32), square_panel, precision=lax.Precis...  2.56 us
  transfers between devices with their start and end apart: 1, of which 1 were waited for; matrix products, arithmetic and copies ran while one was open for 0% of the time, Pallas kernels for 0%

commit v1 on v0

--- a/solution.py
+++ b/solution.py
@@ -55,7 +55,14 @@
         .reshape(height, blocks_total * block_edge)
     )
     square = jnp.dot(row_panel, column_panel, preferred_element_type=jnp.float32)
-    square_panel = lax.all_gather(square, "row", axis=0, tiled=True)
+    x = square
+    ways, here, step = (lax.axis_size("row"), lax.axis_index("row"), x.shape[0])
+    shape = [n * ways if d == 0 else n for d, n in enumerate(x.shape)]
+    full = lax.dynamic_update_slice_in_dim(jnp.zeros(shape, x.dtype), x, here * step, axis=0)
+    for far in range(1, ways):
+        x = lax.ppermute(x, "row", [(d, (d + 1) % ways) for d in range(ways)])
+        full = lax.dynamic_update_slice_in_dim(full, x, (here - far) % ways * step, axis=0)
+    square_panel = full
     cube = jnp.dot(
         row_panel.astype(jnp.float32),
         square_panel,

time: 101 us -> 82.5 us (0.82)
  between operations: 13.6 us -> 0.27 us
  waiting for transfers between devices: 30.9 us -> 24.7 us
  matrix products: 3.83 us -> 1.78 us
  starting transfers between devices: 0.01 us -> 1.93 us
  local copies, waits for them, and re-layouts: 19.6 us -> 21 us
    all_gather x1 -> x0, waiting for transfers between devices: 30.9 us -> none  [on_device(): square_panel = lax.all_gather(square, 'row', axis=0, tiled=True)]
    ppermute x0 -> x3, waiting for transfers between devices: none -> 24.7 us  [on_device(): x = lax.ppermute(x, 'row', [(d, (d + 1) % ways) for d in range(ways)])]
    ppermute x0 -> x3, starting transfers between devices: none -> 1.93 us  [on_device(): x = lax.ppermute(x, 'row', [(d, (d + 1) % ways) for d in range(ways)])]
    dot_general x1, matrix products: 2.56 us -> 1.25 us  [on_device(): jnp.dot(row_panel.astype(jnp.float32), square_panel, precision=lax.Precis...]
  transfers between devices with their start and end apart: 1 -> 3, of which waited for: 1 -> 3; matrix products, arithmetic and copies ran while one was open for 0% -> 0% of each run, Pallas kernels for 0% -> 0%
where the time goes in v1:
time: 82.5 us; the launch traced here: 82.2 us
  blocking collectives  28.8 us (35%)
  waiting for transfers between devices  24.7 us (30%)
  local copies, waits for them, and re-layouts  21 us (25%)
  other arithmetic  3.72 us (5%)
  starting transfers between devices  1.93 us (2%)
  matrix products  1.78 us (2%)
    ppermute x3, waiting for transfers between devices, on_device(): x = lax.ppermute(x, 'row', [(d, (d + 1) % ways) for d in range(ways)])  24.7 us
    all_gather x1, blocking collectives, on_device(): down = lax.all_gather(payload, 'row', axis=0, tiled=False)  16.3 us
    all_gather x1, blocking collectives, on_device(): across = lax.all_gather(payload, 'col', axis=0, tiled=False)  12.4 us
    reshape x1, local copies, waits for them, and re-layouts, on_device(): row_panel = row_grid.reshape(rows_dev, blocks_total, block_edge, block_ed...  3.5 us
    transpose x1, local copies, waits for them, and re-layouts, on_device(): row_panel = row_grid.reshape(rows_dev, blocks_total, block_edge, block_ed...  2.94 us
    reshape x1, local copies, waits for them, and re-layouts, on_device(): row_grid.reshape(rows_dev, blocks_total, block_edge, block_edge)  2.57 us
    another operation x2, other arithmetic  1.94 us
    ppermute x3, starting transfers between devices, on_device(): x = lax.ppermute(x, 'row', [(d, (d + 1) % ways) for d in range(ways)])  1.93 us
  transfers between devices with their start and end apart: 3, of which 3 were waited for; matrix products, arithmetic and copies ran while one was open for 0% of the time, Pallas kernels for 0%

profile of v1, /device:TPU:0, one launch (start us, length us, event | category | flops | bytes accessed | tf_op | source)
XLA Modules:
  0.0 82.2 jit_solution(6766210055116308255)
XLA Ops:
  0.0 0.6 compare_reduce_fusion.4
  0.6 1.3 %broadcast_select_fusion = bf16[1,9]{1,0:T(2,128)(2,1)S(1)} fusion(pred[]{:T(512)} %compare_reduce_fusion.4, s32[1,9]{1,0:T(1,128)} %param.6), kind=kLoop, calls=%fused_computation.38 | loop fusion | flops 18 | bytes 55 | tf_op jit(solution)/shard_map/select.9
  1.9 0.9 %fusion.7 = bf16[1,10,4096]{2,1,0:T(8,128)(2,1)S(1)} fusion(bf16[1,9]{1,0:T(2,128)(2,1)S(1)} %broadcast_select_fusion, bf16[9,4096]{1,0:T(8,128)(2,1)} %bitcast.39), kind=kLoop, calls=%fused_computation.13 | loop fusion | flops 245760 | bytes 155666
  2.9 12.4 %all-gather.2 = bf16[8,10,4096]{2,1,0:T(8,128)(2,1)S(1)} all-gather(bf16[1,10,4096]{2,1,0:T(8,128)(2,1)S(1)} %fusion.7), channel_id=2, replica_groups=mesh['col'=8,'row'=4] {'col'}, dimensions={0}, use_global_device_ids=true | all-gather | bytes 737280 | tf_op jit(solution)/shard_map/all_gather | solution.py:40
  15.4 16.3 %all-gather.3 = bf16[4,10,4096]{2,1,0:T(8,128)(2,1)S(1)} all-gather(bf16[1,10,4096]{2,1,0:T(8,128)(2,1)S(1)} %fusion.7), channel_id=3, replica_groups=mesh['col'=8,'row'=4] {'row'}, dimensions={0}, use_global_device_ids=true | all-gather | bytes 409600 | tf_op jit(solution)/shard_map/all_gather | solution.py:25
  31.7 0.6 compare_reduce_fusion.2
  32.3 0.2 copy-done.1
  32.6 0.1 lt.118
  32.7 0.1 add.165
  32.8 0.1 add.166
  32.8 0.1 rem.96
  32.9 0.1 div.35
  33.0 0.1 ne.118
  33.1 0.3 reshape.316
  33.4 1.8 %scatter_custom_fusion = bf16[144,4096]{1,0:T(8,128)(2,1)S(1)} fusion(s32[72]{0:T(128)S(1)} %fusion.12, bf16[72,4096]{1,0:T(8,128)(2,1)S(1)} %reshape.316, bf16[]{:T(256)} %constant.105.clone.1), kind=kCustom, calls=%fused_computation.5 | custom fusion | bytes 1179650 | tf_op jit(solution)/shard_map/scatter | solution.py:49
  35.2 2.6 %reshape.297 = bf16[6,24,64,64]{3,2,1,0:T(8,128)(2,1)S(1)} reshape(bf16[144,4096]{1,0:T(8,128)(2,1)S(1)} %scatter_custom_fusion) | data formatting | bytes 2359296 | tf_op jit(solution)/shard_map/reshape | solution.py:53
  37.8 2.9 %copy.12 = bf16[6,64,24,64]{3,2,1,0:T(8,128)(2,1)} copy(bf16[6,64,24,64]{3,1,2,0:T(8,128)(2,1)S(1)} %bitcast.34) | data formatting | bytes 2359296 | tf_op jit(solution)/shard_map/transpose | solution.py:54
  40.7 3.5 %reshape.298 = bf16[384,1536]{1,0:T(8,128)(2,1)S(1)} reshape(bf16[6,64,24,64]{3,2,1,0:T(8,128)(2,1)} %copy.12) | data formatting | bytes 2359296 | tf_op jit(solution)/shard_map/reshape | solution.py:55
  44.2 0.0 copy-done.3
  44.2 0.1 lt.123
  44.3 0.1 rem.100
  44.4 0.1 add.171
  44.5 0.1 add.172
  44.6 0.1 div.37
  44.6 0.1 ne.123
  44.7 0.0 copy-done.2
  44.7 0.1 reshape.324
  44.9 1.2 %scatter_custom_fusion.1 = bf16[72,4096]{1,0:T(8,128)(2,1)S(1)} fusion(s32[36]{0:T(128)S(1)} %fusion.13, bf16[36,4096]{1,0:T(8,128)(2,1)S(1)} %reshape.324, bf16[]{:T(256)} %constant.105.clone.1), kind=kCustom, calls=%fused_computation.7 | custom fusion | bytes 589826 | tf_op jit(solution)/shard_map/scatter | solution.py:32
  46.1 1.3 %reshape.300 = bf16[24,3,64,64]{3,2,1,0:T(8,128)(2,1)S(1)} reshape(bf16[72,4096]{1,0:T(8,128)(2,1)S(1)} %scatter_custom_fusion.1) | data formatting | bytes 1179648 | tf_op jit(solution)/shard_map/reshape | solution.py:36
  47.4 1.3 %copy.13 = bf16[24,64,3,64]{1,0,3,2:T(8,128)(2,1)S(1)} copy(bf16[24,64,3,64]{3,1,2,0:T(8,128)(2,1)S(1)} %bitcast.35) | data formatting | bytes 1179648 | tf_op jit(solution)/shard_map/transpose | solution.py:37
  48.7 1.5 %reshape.301 = bf16[1536,192]{0,1:T(8,128)(2,1)} reshape(bf16[24,64,3,64]{1,0,3,2:T(8,128)(2,1)S(1)} %copy.13) | data formatting | bytes 1179648 | tf_op jit(solution)/shard_map/reshape | solution.py:38
  50.2 0.1 broadcast_in_dim.41
  50.3 0.9 %copy-done = bf16[1536,192]{0,1:T(8,128)(2,1)S(1)} copy-done((bf16[1536,192]{0,1:T(8,128)(2,1)S(1)}, bf16[1536,192]{0,1:T(8,128)(2,1)}, u32[]{:S(2)}) %copy-start) | copy-done | bytes 589848
  51.3 0.5 constant_dynamic-update-slice_fusion.3
  51.8 1.9 %collective-permute-start = (f32[384,192]{0,1:T(8,128)S(1)}, f32[384,192]{0,1:T(8,128)S(1)}, u32[]{:S(2)}, u32[]{:S(2)}) collective-permute-start(f32[384,192]{0,1:T(8,128)S(1)} %get-tuple-element.26), channel_id=1, source_target_pairs={{0,1},{1,2},{2,3},{3,0},{4,5},{5,6},{6,7},{7,4},{8,9},{9,10},{10,1... | collective-permute-start | bytes 884744 | tf_op jit(solution)/shard_map/ppermute | solution.py:63
  53.8 7.7 %collective-permute-done = f32[384,192]{0,1:T(8,128)S(1)} collective-permute-done((f32[384,192]{0,1:T(8,128)S(1)}, f32[384,192]{0,1:T(8,128)S(1)}, u32[]{:S(2)}, u32[]{:S(2)}) %collective-permute-start) | collective-permute-done | bytes 294944 | tf_op jit(solution)/shard_map/ppermute | solution.py:63
  61.4 0.0 collective-permute-start.1
  61.4 0.0 copy-done.4
  61.5 8.7 %collective-permute-done.1 = f32[384,192]{0,1:T(8,128)S(1)} collective-permute-done((f32[384,192]{0,1:T(8,128)S(1)}, f32[384,192]{0,1:T(8,128)S(1)}, u32[]{:S(2)}, u32[]{:S(2)}) %collective-permute-start.1) | collective-permute-done | bytes 294944 | tf_op jit(solution)/shard_map/ppermute | solution.py:63
  70.1 0.0 collective-permute-start.2
  70.3 8.4 %collective-permute-done.2 = f32[384,192]{0,1:T(8,128)S(1)} collective-permute-done((f32[384,192]{0,1:T(8,128)S(1)}, f32[384,192]{0,1:T(8,128)S(1)}, u32[]{:S(2)}, u32[]{:S(2)}) %collective-permute-start.2) | collective-permute-done | bytes 294944 | tf_op jit(solution)/shard_map/ppermute | solution.py:63
  78.7 1.2 %fusion = f32[384,192]{0,1:T(8,128)S(1)} fusion(bf16[384,1536]{1,0:T(8,128)(2,1)S(1)} %reshape.298, f32[1536,192]{0,1:T(8,128)S(1)} %constant_dynamic-update-slice_fusion, f32[384,192]{0,1:T(8,128)S(1)} %get-tuple-element.26), kind=kOutput, calls=%fused_computation.4 | convolution fusion | flops 1359175680 | bytes 2949120 | tf_op jit(solution)/shard_map/dot_general | solution.py:66
  79.9 0.2 reshape.302
  80.1 0.3 copy.14
  80.4 0.2 reshape.303
  80.6 0.6 gather_fusion
  81.2 0.1 bitcast_select_fusion
  81.3 0.9 %copy.15 = f32[1,13,4096]{2,0,1:T(1,128)} copy(f32[1,13,4096]{2,1,0:T(8,128)S(1)} %bitcast_select_fusion) | data formatting | bytes 425984 | tf_op jit(solution)/shard_map/jit(_where)/select_n | solution.py:77
  (18 shorter events, 0.3 us)
Async XLA Ops:
  31.7 0.8 copy-start.1
  40.7 3.5 %copy-start.3 = (pred[4,9]{1,0:T(4,128)(4,1)S(1)}, pred[4,9]{1,0:T(4,128)(4,1)}, u32[]{:S(2)}) copy-start(pred[4,9]{1,0:T(4,128)(4,1)} %get-tuple-element.22) | copy-start | bytes 112
  40.7 4.0 %copy-start.2 = (bf16[4,10,4096]{2,1,0:T(8,128)(2,1)S(1)}, bf16[4,10,4096]{2,1,0:T(8,128)(2,1)}, u32[]{:S(2)}) copy-start(bf16[4,10,4096]{2,1,0:T(8,128)(2,1)} %copy-done.1) | copy-start | bytes 983044
  50.2 1.1 %copy-start = (bf16[1536,192]{0,1:T(8,128)(2,1)S(1)}, bf16[1536,192]{0,1:T(8,128)(2,1)}, u32[]{:S(2)}) copy-start(bf16[1536,192]{0,1:T(8,128)(2,1)} %reshape.301) | copy-start | bytes 1769476
  51.3 10.2 %copy-start.4 = (s32[1,13]{1,0:T(1,128)S(1)}, s32[1,13]{1,0:T(1,128)}, u32[]{:S(2)}) copy-start(s32[1,13]{1,0:T(1,128)} %param.7) | copy-start | bytes 160
  51.8 9.6 %collective-permute-start = (f32[384,192]{0,1:T(8,128)S(1)}, f32[384,192]{0,1:T(8,128)S(1)}, u32[]{:S(2)}, u32[]{:S(2)}) collective-permute-start(f32[384,192]{0,1:T(8,128)S(1)} %get-tuple-element.26), channel_id=1, source_target_pairs={{0,1},{1,2},{2,3},{3,0},{4,5},{5,6},{6,7},{7,4},{8,9},{9,10},{10,1... | collective-permute-start | bytes 884744 | tf_op jit(solution)/shard_map/ppermute | solution.py:63
  61.4 8.7 %collective-permute-start.1 = (f32[384,192]{0,1:T(8,128)S(1)}, f32[384,192]{0,1:T(8,128)S(1)}, u32[]{:S(2)}, u32[]{:S(2)}) collective-permute-start(f32[384,192]{0,1:T(8,128)S(1)} %collective-permute-done), channel_id=1, source_target_pairs={{0,1},{1,2},{2,3},{3,0},{4,5},{5,6},{6,7},{7,4},{8,9},{9,10},{10,1... | collective-permute-start | bytes 884744 | tf_op jit(solution)/shard_map/ppermute | solution.py:63
  70.1 8.5 %collective-permute-start.2 = (f32[384,192]{0,1:T(8,128)S(1)}, f32[384,192]{0,1:T(8,128)S(1)}, u32[]{:S(2)}, u32[]{:S(2)}) collective-permute-start(f32[384,192]{0,1:T(8,128)S(1)} %collective-permute-done.1), channel_id=1, source_target_pairs={{0,1},{1,2},{2,3},{3,0},{4,5},{5,6},{6,7},{7,4},{8,9},{9,10},{10,1... | collective-permute-start | bytes 884744 | tf_op jit(solution)/shard_map/ppermute | solution.py:63
